TPU v7x, 512 devices: a whole 4x8x8 slice. The times are simulated.
512 devices in a mesh: row: 64 (over y, x, core), col: 8 (over z).
Axes of the slice: x: 4, y: 8, z: 8, core: 2. Of those that a mesh axis runs over, the one named last changes fastest.
Arguments:
- panel_cols: float32 [16384, 256], P('row'), may hold values from -60 to 60, as said below
- affinity: float32 [16384, 16384], P('row', 'col'), may hold values from -8 to 8, as said below
Outputs:
- updated: float32 [16384, 16384], P('row', 'col')
- band_block: float32 [256, 256], replicated
Inputs may be any that keep to these rules, and one draw needn't show every extreme that they name: affinity holds a symmetric matrix in the stored column order of the steps. panel_cols has full column rank.
All inputs are finite; a program needn't handle non-finite values.
Results may differ from a plain program's by a relative error of at most 0.000071.
Values sent between devices are 32-bit elements; how exact they have to be, the bound alone decides.
No kernel may reach another device: no remote copies, remote signals or barrier semaphores. Data moves between devices by JAX's collectives and lax.ppermute only.
A program may use at most 64 MiB of HBM per device.

v0:
```python
import jax
import jax.numpy as jnp
from jax import lax
from jax.sharding import PartitionSpec as P


def shards(panel_cols, affinity):
    high = lax.Precision.HIGHEST
    local_rows = panel_cols.shape[0]
    piece_rows = local_rows // lax.axis_size("col")
    col_place = lax.axis_index("col")
    gram_sum = lax.psum(jnp.dot(panel_cols.T, panel_cols, precision=high), "row")
    lower_factor = jnp.linalg.cholesky(gram_sum)
    ortho_basis = jax.scipy.linalg.solve_triangular(lower_factor, panel_cols.T, lower=True).T
    own_basis = lax.dynamic_slice_in_dim(ortho_basis, col_place * piece_rows, piece_rows, 0)
    arrived = lax.all_gather(own_basis, "row", axis=0, tiled=True)
    partial_sum = jnp.dot(affinity, arrived, precision=high)
    partial_sum, basis_cols = (partial_sum, arrived)
    moment = lax.psum(partial_sum, "col")
    band_block = lax.psum(jnp.dot(ortho_basis.T, moment, precision=high), "row")
    corrected = moment - 0.5 * jnp.dot(ortho_basis, band_block, precision=high)
    own_corrected = lax.dynamic_slice_in_dim(corrected, col_place * piece_rows, piece_rows, 0)
    update_cols = lax.all_gather(own_corrected, "row", axis=0, tiled=True)
    updated = affinity - jnp.dot(ortho_basis, update_cols.T, precision=high)
    updated = updated - jnp.dot(corrected, basis_cols.T, precision=high)
    return (updated, band_block)


def solution(mesh):
    placed = (P("row", None), P("row", "col"))
    return jax.shard_map(
        shards, mesh=mesh, in_specs=placed, out_specs=(P("row", "col"), P()), check_vma=False
    )
```

profile of v0, /device:TPU:1, one launch (start us, length us, event | category | flops | bytes accessed | tf_op | source)
XLA Modules:
  0.0 722.9 jit_solution(2886932835697183772)
XLA Ops:
  7.2 0.0 all-reduce.5.cloned.1.call-start
  7.2 2.3 fusion.16
  9.5 0.0 copy-start.2
  9.5 0.0 all-reduce.5.cloned.1.call-update
  9.6 0.0 all-gather.3.cloned.1.call-start
  9.6 196.8 %all-reduce.5.cloned.1.call-done = f32[256,256]{0,1:T(8,128)} async-done(((f32[256,256]{0,1:T(8,128)}), f32[256,256]{0,1:T(8,128)}) %all-reduce.5.cloned.1.call-update) | async-done | bytes 262160 | tf_op jit(solution)/shard_map/psum | solution.py:12
  206.4 1.1 copy.8
  207.5 1.0 fusion.1
  208.5 11.7 %cholesky.50 = f32[128,128]{1,0:T(8,128)S(1)} custom-call(f32[128,128]{1,0:T(8,128)S(1)} %cholesky.118), custom_call_target="Cholesky" | custom-call | tf_op jit(solution)/shard_map/jit(cholesky)/cholesky | solution.py:13
  220.2 0.0 copy-start
  220.3 9.8 %custom-call.15 = f32[1,128,128]{1,2,0:T(8,128)S(1)} custom-call(f32[1,128,128]{2,1,0:T(8,128)S(1)} %get-tuple-element.23), custom_call_target="InvertDiagBlocksLowerTriangular" | custom-call | tf_op jit(solution)/shard_map/jit(cholesky)/cholesky | solution.py:13
  230.1 0.2 constant_dynamic-update-slice_fusion
  230.3 0.3 convolution_subtract_fusion.3
  230.6 11.7 %cholesky.105 = f32[128,128]{1,0:T(8,128)S(1)} custom-call(f32[128,128]{1,0:T(8,128)S(1)} %convolution_subtract_fusion.3), custom_call_target="Cholesky" | custom-call | tf_op jit(solution)/shard_map/jit(cholesky)/cholesky | solution.py:13
  242.3 0.7 compare_reduce_fusion
  244.3 0.1 triangular_solve.57
  244.4 4.1 while.1
  244.5 0.6 fusion.31
  245.1 1.4 bitcast_dynamic-update-slice_fusion.2
  246.5 0.6 fusion.31
  247.1 1.4 bitcast_dynamic-update-slice_fusion.2
  248.5 19.7 %custom-call.16 = f32[2,128,128]{1,2,0:T(8,128)S(1)} custom-call(f32[2,128,128]{2,1,0:T(8,128)S(1)} %get-tuple-element.9), custom_call_target="InvertDiagBlocksLowerTriangular" | custom-call | tf_op jit(solution)/shard_map/jit(_solve_triangular)/triangular_solve | solution.py:14
  268.1 0.0 copy-done.2
  268.1 0.3 fusion.5
  268.5 0.4 convolution_subtract_fusion.2
  268.9 0.3 fusion.8
  269.2 0.1 fusion.4
  269.3 0.7 copy.9
  270.0 0.0 all-gather.3.cloned.1.call-update
  270.0 0.0 all-reduce.7.cloned.1.call-start
  270.1 80.7 %all-gather.3.cloned.1.call-done = f32[2048,256]{1,0:T(8,128)} async-done(((f32[32,256]{1,0:T(8,128)}), f32[2048,256]{1,0:T(8,128)}) %all-gather.3.cloned.1.call-update) | async-done | bytes 2097168 | tf_op jit(solution)/shard_map/all_gather | solution.py:16
  350.7 0.0 copy-done
  350.7 4.2 convolution_bitcast_fusion
  355.0 0.0 all-reduce.7.cloned.1.call-update
  355.0 0.0 all-reduce.9.cloned.1.call-start
  355.0 71.6 %all-reduce.7.cloned.1.call-done = f32[256,256]{1,0:T(8,128)} async-done(((f32[256,256]{1,0:T(8,128)}), f32[256,256]{1,0:T(8,128)}) %all-reduce.7.cloned.1.call-update) | async-done | bytes 262160 | tf_op jit(solution)/shard_map/psum | solution.py:19
  426.6 2.0 fusion.2
  428.7 0.0 all-reduce.9.cloned.1.call-update
  428.7 0.0 all-gather.5.cloned.1.call-start
  428.7 193.9 %all-reduce.9.cloned.1.call-done = f32[256,256]{1,0:T(8,128)} async-done(((f32[256,256]{1,0:T(8,128)}), f32[256,256]{1,0:T(8,128)}) %all-reduce.9.cloned.1.call-update) | async-done | bytes 262160 | tf_op jit(solution)/shard_map/psum | solution.py:20
  622.6 1.6 fusion
  624.2 0.6 constant_dynamic-slice_fusion.1
  624.9 0.0 all-gather.5.cloned.1.call-update
  624.9 82.1 %all-gather.5.cloned.1.call-done = f32[2048,256]{1,0:T(8,128)} async-done(((f32[32,256]{1,0:T(8,128)}), f32[2048,256]{1,0:T(8,128)}) %all-gather.5.cloned.1.call-update) | async-done | bytes 2097168 | tf_op jit(solution)/shard_map/all_gather | solution.py:23
  707.0 0.0 copy-start.1
  707.0 5.3 convolution_subtract_fusion.1
  712.2 0.0 copy-done.1
  712.2 0.0 copy-start.3
  712.3 3.4 convolution_subtract_fusion
  715.6 0.0 copy-done.3
  715.6 0.7 copy.26
  (9 shorter events, 0.1 us)
Async XLA Ops:
  7.2 199.3 %all-reduce.5.cloned.1.call-start = ((), (), s32[]{:S(2)}) async-start(), calls=%async_computation | async-start | bytes 524288 | tf_op jit(solution)/shard_map/psum | solution.py:12
  9.5 258.6 %copy-start.2 = (f32[256,256]{1,0:T(8,128)S(1)}, f32[256,256]{1,0:T(8,128)}, u32[]{:S(2)}) copy-start(f32[256,256]{1,0:T(8,128)} %param.2) | copy-start | bytes 786436
  9.6 341.1 %all-gather.3.cloned.1.call-start = ((), (), s32[]{:S(2)}) async-start(), calls=%async_computation.1 | async-start | bytes 2129920 | tf_op jit(solution)/shard_map/all_gather | solution.py:16
  220.2 130.5 %copy-start = (f32[256,2048]{1,0:T(8,128)S(1)}, f32[256,2048]{1,0:T(8,128)}, u32[]{:S(2)}) copy-start(f32[256,2048]{1,0:T(8,128)} %param.3) | copy-start | bytes 6291460
  270.0 156.6 %all-reduce.7.cloned.1.call-start = ((), (), s32[]{:S(2)}) async-start(), calls=%async_computation.2 | async-start | bytes 524288 | tf_op jit(solution)/shard_map/psum | solution.py:19
  355.0 267.6 %all-reduce.9.cloned.1.call-start = ((), (), s32[]{:S(2)}) async-start(), calls=%async_computation.3 | async-start | bytes 524288 | tf_op jit(solution)/shard_map/psum | solution.py:20
  428.7 278.3 %all-gather.5.cloned.1.call-start = ((), (), s32[]{:S(2)}) async-start(), calls=%async_computation.4 | async-start | bytes 2129920 | tf_op jit(solution)/shard_map/all_gather | solution.py:23
  707.0 5.3 copy-start.1
  712.2 3.4 copy-start.3
Sparse Core Ops, SparseCore 0:
  12.0 194.3 all-reduce.4
  270.1 80.5 all-gather.2
  355.1 71.4 all-reduce.6
  430.5 192.0 all-reduce.8
  626.4 80.5 all-gather.4
where the time goes:
time: 723 us
  waiting for transfers between devices  625 us (86%)
  other arithmetic  54.8 us (8%)
  matrix products  20.3 us (3%)
  between operations  15.2 us (2%)
    psum x1, waiting for transfers between devices, shards(): lax.psum(jnp.dot(panel_cols.T, panel_cols, precision=high), 'row')  197 us
    psum x1, waiting for transfers between devices, shards(): band_block = lax.psum(jnp.dot(ortho_basis.T, moment, precision=high), 'row')  194 us
    all_gather x1, waiting for transfers between devices, shards(): update_cols = lax.all_gather(own_corrected, 'row', axis=0, tiled=True)  82.1 us
    all_gather x1, waiting for transfers between devices, shards(): arrived = lax.all_gather(own_basis, 'row', axis=0, tiled=True)  80.7 us
    psum x1, waiting for transfers between devices, shards(): moment = lax.psum(partial_sum, 'col')  71.6 us
    another operation x6, other arithmetic, shards(): lower_factor = jnp.linalg.cholesky(gram_sum)  34 us
    another operation x3, other arithmetic, shards(): jax.scipy.linalg.solve_triangular(lower_factor, panel_cols.T, lower=True)  19.7 us
  transfers between devices with their start and end apart: 5, of which 5 were waited for; matrix products, arithmetic and copies ran while one was open for 0% of the time, Pallas kernels for 0%

commit v1 on v0

--- a/solution.py
+++ b/solution.py
@@ -16,7 +16,9 @@
     arrived = lax.all_gather(own_basis, "row", axis=0, tiled=True)
     partial_sum = jnp.dot(affinity, arrived, precision=high)
     partial_sum, basis_cols = (partial_sum, arrived)
-    moment = lax.psum(partial_sum, "col")
+    moment = partial_sum
+    for hop in (1, 2, 4):
+        moment = moment + lax.ppermute(moment, "col", [(dev, dev ^ hop) for dev in range(8)])
     band_block = lax.psum(jnp.dot(ortho_basis.T, moment, precision=high), "row")
     corrected = moment - 0.5 * jnp.dot(ortho_basis, band_block, precision=high)
     own_corrected = lax.dynamic_slice_in_dim(corrected, col_place * piece_rows, piece_rows, 0)

time: 723 us -> 685 us (0.947)
  waiting for transfers between devices: 625 us -> 573 us
  starting transfers between devices: 0.21 us -> 16.5 us
    psum x1 -> x0, waiting for transfers between devices: 71.6 us -> none  [shards(): moment = lax.psum(partial_sum, 'col')]
    ppermute x0 -> x3, waiting for transfers between devices: none -> 29.1 us  [shards(): lax.ppermute(moment, 'col', [(dev, dev ^ hop) for dev in range(8)])]
    ppermute x0 -> x3, starting transfers between devices: none -> 16.2 us  [shards(): lax.ppermute(moment, 'col', [(dev, dev ^ hop) for dev in range(8)])]
    psum x1, waiting for transfers between devices: 194 us -> 184 us  [shards(): band_block = lax.psum(jnp.dot(ortho_basis.T, moment, precision=high), 'row')]
  transfers between devices with their start and end apart: 5 -> 7, of which waited for: 5 -> 7; matrix products, arithmetic and copies ran while one was open for 0% -> 0% of each run, Pallas kernels for 0% -> 0%
where the time goes in v1:
time: 685 us
  waiting for transfers between devices  573 us (84%)
  other arithmetic  54.8 us (8%)
  matrix products  18.6 us (3%)
  starting transfers between devices  16.5 us (2%)
  between operations  15.2 us (2%)
  local copies, waits for them, and re-layouts  6.99 us (1%)
    psum x1, waiting for transfers between devices, shards(): lax.psum(jnp.dot(panel_cols.T, panel_cols, precision=high), 'row')  197 us
    psum x1, waiting for transfers between devices, shards(): band_block = lax.psum(jnp.dot(ortho_basis.T, moment, precision=high), 'row')  184 us
    all_gather x1, waiting for transfers between devices, shards(): update_cols = lax.all_gather(own_corrected, 'row', axis=0, tiled=True)  82.2 us
    all_gather x1, waiting for transfers between devices, shards(): arrived = lax.all_gather(own_basis, 'row', axis=0, tiled=True)  80.7 us
    another operation x6, other arithmetic, shards(): lower_factor = jnp.linalg.cholesky(gram_sum)  33.9 us
    ppermute x3, waiting for transfers between devices, shards(): lax.ppermute(moment, 'col', [(dev, dev ^ hop) for dev in range(8)])  29.1 us
    another operation x3, other arithmetic, shards(): jax.scipy.linalg.solve_triangular(lower_factor, panel_cols.T, lower=True)  19.7 us
    ppermute x3, starting transfers between devices, shards(): lax.ppermute(moment, 'col', [(dev, dev ^ hop) for dev in range(8)])  16.2 us
  transfers between devices with their start and end apart: 7, of which 7 were waited for; matrix products, arithmetic and copies ran while one was open for 0% of the time, Pallas kernels for 0%

profile of v1, /device:TPU:1, one launch (start us, length us, event | category | flops | bytes accessed | tf_op | source)
XLA Modules:
  0.0 685.1 jit_solution(11867380836916276557)
XLA Ops:
  7.2 0.0 all-reduce.4.cloned.1.call-start
  7.2 2.3 fusion.16
  9.5 0.0 copy-start.2
  9.5 0.0 all-reduce.4.cloned.1.call-update
  9.6 0.0 all-gather.3.cloned.1.call-start
  9.6 196.8 %all-reduce.4.cloned.1.call-done = f32[256,256]{0,1:T(8,128)} async-done(((f32[256,256]{0,1:T(8,128)}), f32[256,256]{0,1:T(8,128)}) %all-reduce.4.cloned.1.call-update) | async-done | bytes 262160 | tf_op jit(solution)/shard_map/psum | solution.py:12
  206.4 1.1 copy.7
  207.5 1.0 fusion.1
  208.5 11.7 %cholesky.50 = f32[128,128]{1,0:T(8,128)S(1)} custom-call(f32[128,128]{1,0:T(8,128)S(1)} %cholesky.118), custom_call_target="Cholesky" | custom-call | tf_op jit(solution)/shard_map/jit(cholesky)/cholesky | solution.py:13
  220.2 0.0 copy-start
  220.3 9.8 %custom-call.15 = f32[1,128,128]{1,2,0:T(8,128)S(1)} custom-call(f32[1,128,128]{2,1,0:T(8,128)S(1)} %get-tuple-element.23), custom_call_target="InvertDiagBlocksLowerTriangular" | custom-call | tf_op jit(solution)/shard_map/jit(cholesky)/cholesky | solution.py:13
  230.1 0.2 constant_dynamic-update-slice_fusion
  230.3 0.3 convolution_subtract_fusion.3
  230.6 11.7 %cholesky.105 = f32[128,128]{1,0:T(8,128)S(1)} custom-call(f32[128,128]{1,0:T(8,128)S(1)} %convolution_subtract_fusion.3), custom_call_target="Cholesky" | custom-call | tf_op jit(solution)/shard_map/jit(cholesky)/cholesky | solution.py:13
  242.3 0.6 compare_reduce_fusion
  244.2 0.1 triangular_solve.57
  244.3 4.0 while.1
  244.5 0.6 fusion.31
  245.0 1.3 bitcast_dynamic-update-slice_fusion.2
  246.4 0.6 fusion.31
  247.0 1.3 bitcast_dynamic-update-slice_fusion.2
  248.3 19.7 %custom-call.16 = f32[2,128,128]{1,2,0:T(8,128)S(1)} custom-call(f32[2,128,128]{2,1,0:T(8,128)S(1)} %get-tuple-element.9), custom_call_target="InvertDiagBlocksLowerTriangular" | custom-call | tf_op jit(solution)/shard_map/jit(_solve_triangular)/triangular_solve | solution.py:14
  267.9 0.0 copy-done.2
  268.0 0.3 fusion.5
  268.3 0.4 convolution_subtract_fusion.2
  268.7 0.3 fusion.8
  269.0 0.1 fusion.4
  269.1 0.7 copy.8
  269.8 0.0 all-gather.3.cloned.1.call-update
  269.8 0.0 all-reduce.6.cloned.1.call-start
  269.9 80.7 %all-gather.3.cloned.1.call-done = f32[2048,256]{1,0:T(8,128)} async-done(((f32[32,256]{1,0:T(8,128)}), f32[2048,256]{1,0:T(8,128)}) %all-gather.3.cloned.1.call-update) | async-done | bytes 2097168 | tf_op jit(solution)/shard_map/all_gather | solution.py:16
  350.5 0.0 copy-done
  350.5 3.5 convolution_bitcast_fusion
  354.1 3.3 collective-permute-start
  357.3 6.2 collective-permute-done
  363.6 4.3 collective-permute-start.1
  367.9 11.3 %collective-permute-done.1 = f32[256,256]{1,0:T(8,128)S(1)} collective-permute-done((f32[256,256]{1,0:T(8,128)S(1)}, f32[256,256]{1,0:T(8,128)S(1)}, u32[]{:S(2)}, u32[]{:S(2)}) %collective-permute-start.1) | collective-permute-done | bytes 262176 | tf_op jit(solution)/shard_map/ppermute | solution.py:21
  379.3 8.5 %collective-permute-start.2 = (f32[256,256]{1,0:T(8,128)S(1)}, f32[256,256]{1,0:T(8,128)S(1)}, u32[]{:S(2)}, u32[]{:S(2)}) collective-permute-start(f32[256,256]{1,0:T(8,128)S(1)} %add.43), channel_id=1, source_target_pairs={{0,4},{1,5},{2,6},{3,7},{4,0},{5,1},{6,2},{7,3},{8,12},{9,13},{10,... | collective-permute-start | bytes 786440 | tf_op jit(solution)/shard_map/ppermute | solution.py:21
  387.8 11.6 %collective-permute-done.2 = f32[256,256]{1,0:T(8,128)S(1)} collective-permute-done((f32[256,256]{1,0:T(8,128)S(1)}, f32[256,256]{1,0:T(8,128)S(1)}, u32[]{:S(2)}, u32[]{:S(2)}) %collective-permute-start.2) | collective-permute-done | bytes 262176 | tf_op jit(solution)/shard_map/ppermute | solution.py:21
  399.4 1.1 fusion.2
  400.5 0.0 all-reduce.6.cloned.1.call-update
  400.6 0.3 all-gather.5.cloned.1.call-start
  400.8 184.0 %all-reduce.6.cloned.1.call-done = f32[256,256]{1,0:T(8,128)} async-done(((f32[256,256]{1,0:T(8,128)}), f32[256,256]{1,0:T(8,128)}) %all-reduce.6.cloned.1.call-update) | async-done | bytes 262160 | tf_op jit(solution)/shard_map/psum | solution.py:22
  584.8 1.5 fusion
  586.4 0.6 constant_dynamic-slice_fusion.1
  587.0 0.0 all-gather.5.cloned.1.call-update
  587.0 82.2 %all-gather.5.cloned.1.call-done = f32[2048,256]{1,0:T(8,128)} async-done(((f32[32,256]{1,0:T(8,128)}), f32[2048,256]{1,0:T(8,128)}) %all-gather.5.cloned.1.call-update) | async-done | bytes 2097168 | tf_op jit(solution)/shard_map/all_gather | solution.py:25
  669.2 0.0 copy-start.1
  669.2 5.3 convolution_subtract_fusion.1
  674.5 0.0 copy-done.1
  674.5 0.0 copy-start.3
  674.5 3.4 convolution_subtract_fusion
  677.8 0.0 copy-done.3
  677.8 0.7 copy.22
  (12 shorter events, 0.2 us)
Async XLA Ops:
  7.2 199.3 %all-reduce.4.cloned.1.call-start = ((), (), s32[]{:S(2)}) async-start(), calls=%async_computation | async-start | bytes 524288 | tf_op jit(solution)/shard_map/psum | solution.py:12
  9.5 258.4 %copy-start.2 = (f32[256,256]{1,0:T(8,128)S(1)}, f32[256,256]{1,0:T(8,128)}, u32[]{:S(2)}) copy-start(f32[256,256]{1,0:T(8,128)} %param.2) | copy-start | bytes 786436
  9.6 340.9 %all-gather.3.cloned.1.call-start = ((), (), s32[]{:S(2)}) async-start(), calls=%async_computation.1 | async-start | bytes 2129920 | tf_op jit(solution)/shard_map/all_gather | solution.py:16
  220.2 130.3 %copy-start = (f32[256,2048]{1,0:T(8,128)S(1)}, f32[256,2048]{1,0:T(8,128)}, u32[]{:S(2)}) copy-start(f32[256,2048]{1,0:T(8,128)} %param.3) | copy-start | bytes 6291460
  269.8 315.0 %all-reduce.6.cloned.1.call-start = ((), (), s32[]{:S(2)}) async-start(), calls=%async_computation.2 | async-start | bytes 524288 | tf_op jit(solution)/shard_map/psum | solution.py:22
  354.1 9.5 %collective-permute-start = (f32[256,256]{1,0:T(8,128)S(1)}, f32[256,256]{1,0:T(8,128)S(1)}, u32[]{:S(2)}, u32[]{:S(2)}) collective-permute-start(f32[256,256]{1,0:T(8,128)S(1)} %convolution_bitcast_fusion), channel_id=1, source_target_pairs={{0,1},{1,0},{2,3},{3,2},{4,5},{5,4},{6,7},{7,6},{8,9},{9,8},{10,11... | collective-permute-start | bytes 786440 | tf_op jit(solution)/shard_map/ppermute | solution.py:21
  363.6 15.6 %collective-permute-start.1 = (f32[256,256]{1,0:T(8,128)S(1)}, f32[256,256]{1,0:T(8,128)S(1)}, u32[]{:S(2)}, u32[]{:S(2)}) collective-permute-start(f32[256,256]{1,0:T(8,128)S(1)} %add.42), channel_id=1, source_target_pairs={{0,2},{1,3},{2,0},{3,1},{4,6},{5,7},{6,4},{7,5},{8,10},{9,11},{10,... | collective-permute-start | bytes 786440 | tf_op jit(solution)/shard_map/ppermute | solution.py:21
  379.3 20.1 %collective-permute-start.2 = (f32[256,256]{1,0:T(8,128)S(1)}, f32[256,256]{1,0:T(8,128)S(1)}, u32[]{:S(2)}, u32[]{:S(2)}) collective-permute-start(f32[256,256]{1,0:T(8,128)S(1)} %add.43), channel_id=1, source_target_pairs={{0,4},{1,5},{2,6},{3,7},{4,0},{5,1},{6,2},{7,3},{8,12},{9,13},{10,... | collective-permute-start | bytes 786440 | tf_op jit(solution)/shard_map/ppermute | solution.py:21
  400.6 268.6 %all-gather.5.cloned.1.call-start = ((), (), s32[]{:S(2)}) async-start(), calls=%async_computation.3 | async-start | bytes 2129920 | tf_op jit(solution)/shard_map/all_gather | solution.py:25
  669.2 5.3 copy-start.1
  674.5 3.4 copy-start.3
Sparse Core Ops, SparseCore 0:
  12.0 194.3 all-reduce.3
  269.9 80.5 all-gather.2
  400.7 184.1 all-reduce.5
  588.6 80.5 all-gather.4
